TPU v7x, 128 devices: a whole 4x4x4 slice. The times are simulated.
128 devices in a mesh: pix: 8 (over y_hi, z), tm: 16 (over x, y_lo, core).
Axes of the slice: x: 4, y: 4 (y_hi: 2, y_lo: 2; y = y_hi * 2 + y_lo), z: 4, core: 2. Of those that a mesh axis runs over, the one named last changes fastest.
Arguments:
- frames: float32 [16, 192, 12288], P('tm', 'pix'), may hold values from 0.05 to 5
- pixel_order: int32 [12288], replicated, may hold values from 0 to 12287, each once
- cycle_sizes: int32 [64], replicated, may hold values from 1 to 384, 12288 in all
- kernel: float32 [5], replicated, may hold values from 0.1 to 1
Outputs:
- correlation: float32 [64, 3072, 3072], P('pix', 'tm')
Inputs may be any that keep to these rules, and one draw needn't show every extreme that they name: `cycle_sizes`: every cycle has one or more pixels, the sizes sum to 12288, and one cycle has exactly 384.
All inputs are finite; a program needn't handle non-finite values.
Results may differ from a plain program's by a relative error of at most 0.00005.
Values sent between devices are 32-bit elements; how exact they have to be, the bound alone decides.
No kernel may reach another device: no remote copies, remote signals or barrier semaphores. Data moves between devices by JAX's collectives and lax.ppermute only.
A program may use at most 256 MiB of HBM per device.

v0:
```python
import jax
import jax.numpy as jnp
from jax import lax
from jax.sharding import Mesh
from jax.sharding import PartitionSpec as P

REACH = 2
PIX = ("yh", "z")
TM = ("x", "yl", "c")
CHIPS = ("x", "yl")


def halo_frames(block, width):
    count = lax.axis_size(TM)
    forward = [(i, i + 1) for i in range(count - 1)]
    backward = [(i + 1, i) for i in range(count - 1)]
    n = block.shape[-1]
    low = lax.ppermute(block[..., n - width :], TM, forward)
    high = lax.ppermute(block[..., :width], TM, backward)
    return jnp.concatenate([low, block, high], axis=-1)


def correlate(left, right):
    return jnp.einsum(
        "rfs,rgs->rfg",
        left,
        right,
        precision=lax.Precision.HIGH,
        preferred_element_type=jnp.float32,
    )


def per_device(frames, pixel_order, cycle_sizes, kernel):
    block = frames[0]
    sub, pixels = block.shape
    cycles = cycle_sizes.shape[0]
    cap = 2 * pixels // cycles
    groups = lax.axis_size(PIX)
    owned = cycles // groups
    half = owned // 2
    window = owned * cap
    starts = (jnp.cumsum(cycle_sizes) - cycle_sizes).astype(jnp.int32)
    me = lax.axis_index(PIX)
    ordered = jnp.take(block.T, pixel_order, axis=0)
    ordered = jnp.pad(ordered, ((0, window), (0, 0)))
    chunks = jnp.stack(
        [lax.dynamic_slice_in_dim(ordered, starts[d * owned], window, 0) for d in range(groups)]
    )
    got = lax.all_to_all(chunks, PIX, 0, 0, tiled=True)
    got = jnp.pad(got, ((0, 0), (0, cap), (0, 0)))
    base = starts[me * owned]
    slots = jnp.arange(cap, dtype=jnp.int32)
    picked = []
    for l in range(owned):
        r = me * owned + l
        rows = lax.dynamic_slice_in_dim(got, starts[r] - base, cap, 1)
        picked.append(jnp.where((slots < cycle_sizes[r])[None, :, None], rows, 0.0))
    picked = jnp.stack(picked)
    picked = jnp.transpose(picked, (0, 2, 1, 3)).reshape(owned, cap, groups * sub)
    tblk = groups * sub
    total = jnp.sum(picked, axis=1, keepdims=True)
    scaled = picked / total
    rimmed = halo_frames(scaled, REACH)
    smooth = kernel[0] * rimmed[..., 0:tblk]
    for shift_step in range(1, 2 * REACH + 1):
        smooth = smooth + kernel[shift_step] * rimmed[..., shift_step : shift_step + tblk]
    smooth = jnp.swapaxes(smooth, 1, 2)
    core = lax.axis_index("c")
    keep = lax.dynamic_slice_in_dim(smooth, core * half, half, 0)
    give = lax.dynamic_slice_in_dim(smooth, (1 - core) * half, half, 0)
    other = lax.ppermute(give, "c", [(0, 1), (1, 0)])
    pair = jnp.where(
        core == 0, jnp.concatenate([keep, other], 1), jnp.concatenate([other, keep], 1)
    )
    right = lax.all_gather(pair, CHIPS, axis=1, tiled=True)
    scale = lax.dynamic_slice_in_dim(cycle_sizes, me * owned + core * half, half).astype(
        jnp.float32
    )
    scale = scale[:, None, None]
    sent = correlate(other * scale, right)
    back = lax.ppermute(sent, "c", [(0, 1), (1, 0)])
    mine = correlate(keep * scale, right)
    return jnp.where(core == 0, jnp.concatenate([mine, back], 0), jnp.concatenate([back, mine], 0))


def solution(mesh):
    pix, tm = (mesh.shape["pix"], mesh.shape["tm"])
    fine = Mesh(mesh.devices.reshape(2, pix // 2, tm // 4, 2, 2), PIX + TM)
    placed = (P(TM, PIX, None), P(), P(), P())
    return jax.shard_map(
        per_device, mesh=fine, in_specs=placed, out_specs=P(PIX, TM, None), check_vma=False
    )
```

profile of v0, /device:TPU:1, one launch (start us, length us, event | category | flops | bytes accessed | tf_op | source)
XLA Modules:
  0.0 593.9 jit_solution(16584004930738798835)
XLA Ops:
  6.5 0.7 copy.8
  7.3 0.1 reduce-window.9
  7.4 0.1 reduce.1
  7.5 0.7 sub.49
  8.2 1.7 fusion.42
  19.8 0.8 compare_and_fusion
  20.6 0.8 fusion.39
  21.5 4.9 copy.7
  31.3 43.9 %gather_fusion = f32[12288,24]{1,0:T(8,128)} fusion(f32[12288,24]{1,0:T(8,128)} %bitcast.91, s32[12288]{0:T(1024)S(1)} %fusion.39), kind=kCustom, calls=%fused_computation | custom fusion | bytes 2408448 | tf_op jit(solution)/shard_map/jit(_take)/gather | solution.py:44
  75.2 8.6 %broadcast_select_fusion = f32[12288,24]{1,0:T(8,128)S(1)} fusion(f32[12288,24]{1,0:T(8,128)} %gather_fusion, pred[12288]{0:T(1024)(128)(4,1)S(1)} %compare_and_fusion), kind=kLoop, calls=%fused_computation.10 | loop fusion | flops 294912 | bytes 2371584 | tf_op jit(solution)/shard_map/jit(_take)/select_n | solution.py:44
  83.8 7.3 %pad_dynamic-slice_fusion = (f32[3072,24]{1,0:T(8,128)}, f32[3072,24]{1,0:T(8,128)}, f32[3072,24]{1,0:T(8,128)}, f32[3072,24]{1,0:T(8,128)}, f32[3072,24]{1,0:T(...) fusion(s32[]{:T(128)S(6)} %select_n.149, f32[12288,24]{1,0:T(8,128)S(1)} %broadcast_select_fusion, ...), kind=kLoop, calls=%fused_computation.2 | loop fusion | bytes 3538976 | tf_op jit(solution)/shard_map/dynamic_slice | solution.py:47
  91.1 2.0 copy.16
  93.1 2.6 copy.10
  95.6 1.2 copy.11
  96.8 1.2 copy.12
  98.0 2.7 copy.13
  100.7 2.6 copy.14
  103.3 1.1 copy.15
  104.4 1.2 copy.9
  105.6 1.7 bitcast_dynamic-update-slice_fusion.7
  107.3 1.7 bitcast_dynamic-update-slice_fusion.6
  109.0 0.7 bitcast_dynamic-update-slice_fusion.5
  109.7 0.7 bitcast_dynamic-update-slice_fusion.4
  110.5 0.7 bitcast_dynamic-update-slice_fusion.3
  111.2 0.7 bitcast_dynamic-update-slice_fusion.2
  111.9 0.7 bitcast_dynamic-update-slice_fusion.1
  112.7 0.7 bitcast_dynamic-update-slice_fusion
  113.4 8.5 %all-to-all-start = ((f32[8,3072,24]{1,2,0:T(8,128)}), f32[8,3072,24]{1,2,0:T(8,128)S(1)}, u32[]{:S(2)}, u32[]{:S(2)}) async-start(f32[8,3072,24]{1,2,0:T(8,128)} %bitcast_dynamic-update-slice_fusion), calls=%async_computation | async-start | bytes 4718592 | tf_op jit(solution)/shard_map/all_to_all | solution.py:49
  130.8 0.6 iota_compare_fusion
  131.4 0.5 iota_compare_fusion.1
  131.9 0.6 iota_compare_fusion.2
  132.5 0.6 iota_compare_fusion.3
  133.2 0.6 iota_compare_fusion.4
  133.8 0.7 iota_compare_fusion.5
  134.5 0.6 iota_compare_fusion.6
  135.1 0.6 iota_compare_fusion.7
  135.7 15.2 %all-to-all-done = f32[8,3072,24]{1,2,0:T(8,128)S(1)} async-done(((f32[8,3072,24]{1,2,0:T(8,128)}), f32[8,3072,24]{1,2,0:T(8,128)S(1)}, u32[]{:S(2)}, u32[]{:S(2)}) %all-to-all-start) | async-done | bytes 2359328 | tf_op jit(solution)/shard_map/all_to_all | solution.py:49
  150.9 0.2 fusion.18
  151.1 0.2 fusion.21
  151.2 0.2 fusion.24
  151.4 0.2 fusion.27
  151.6 0.2 fusion.30
  151.7 0.2 fusion.33
  151.9 0.2 fusion.36
  152.1 1.4 copy-done
  153.5 0.3 bitcast_reduce_fusion
  153.8 2.0 bitcast_divide_fusion
  155.8 3.4 collective-permute-start
  159.2 1.9 collective-permute-start.1
  161.1 0.7 fusion.41
  161.8 2.5 collective-permute-done.1
  164.3 4.7 fusion.3
  169.0 0.2 dynamic-slice_bitcast_fusion.1
  169.2 0.3 collective-permute-start.2
  169.5 2.8 collective-permute-done.2
  172.3 1.6 maximum_select_fusion.1
  173.9 0.6 copy-done.10
  174.5 0.1 dynamic-slice_convert_fusion
  174.6 364.7 %all-gather.2.cloned.1.call-done = f32[4,3072,384]{2,1,0:T(8,128)} async-done(((f32[4,384,384]{2,1,0:T(8,128)}), f32[4,3072,384]{2,1,0:T(8,128)}) %all-gather.2.cloned.1.call-update) | async-done | bytes 18874384 | tf_op jit(solution)/shard_map/all_gather | solution.py:75
  539.3 16.5 %fusion.10 = f32[4,192,3072]{2,1,0:T(8,128)} fusion(f32[4,3072,384]{2,1,0:T(8,128)} %all-gather.2.cloned.1.call-done, f32[4,192,384]{2,1,0:T(8,128)S(1)} %collective-permute-done.2, f32[4]{0:T(128)S(1)} %dynamic-slice_convert_fusion), kind=kOutput, calls=%fused_computation.37 | convolution fusion | flops 5436112896 | bytes 29491216 | tf_op jit(solution)/shard_map/rfs,rgs->rfg/dot_general | solution.py:24
  555.8 0.8 collective-permute-start.3
  556.7 13.6 %fusion.12 = f32[4,192,3072]{2,1,0:T(8,128)S(1)} fusion(f32[4,3072,384]{2,1,0:T(8,128)} %all-gather.2.cloned.1.call-done, f32[4,192,384]{2,1,0:T(8,128)S(1)} %get-tuple-element.13, f32[4]{0:T(128)S(1)} %dynamic-slice_convert_fusion), kind=kOutput, calls=%fused_computation.40 | convolution fusion | flops 5436112896 | bytes 29491216 | tf_op jit(solution)/shard_map/rfs,rgs->rfg/dot_general | solution.py:24
  570.2 1.0 collective-permute-done.3
  571.3 15.7 %maximum_select_fusion = f32[8,192,3072]{2,1,0:T(8,128)} fusion(f32[4,192,3072]{2,1,0:T(8,128)} %collective-permute-done.3, f32[4,192,3072]{2,1,0:T(8,128)S(1)} %fusion.12, pred[]{:T(512)S(6)} %eq.4), kind=kLoop, calls=%fused_computation.1 | loop fusion | flops 14155776 | bytes 37748736 | tf_op jit(solution)/shard_map/jit(_where)/select_n | solution.py:83
  (28 shorter events, 0.2 us)
Async XLA Ops:
  91.1 4.6 copy-start.4
  91.1 5.8 copy-start.3
  96.8 6.4 %copy-start.2 = (f32[3072,24]{1,0:T(8,128)S(1)}, f32[3072,24]{1,0:T(8,128)}, u32[]{:S(2)}) copy-start(f32[3072,24]{1,0:T(8,128)} %get-tuple-element.11) | copy-start | bytes 884740
  98.0 6.4 %copy-start.1 = (f32[3072,24]{1,0:T(8,128)S(1)}, f32[3072,24]{1,0:T(8,128)}, u32[]{:S(2)}) copy-start(f32[3072,24]{1,0:T(8,128)} %get-tuple-element.12) | copy-start | bytes 884740
  104.4 4.6 copy-start.9
  104.4 5.3 copy-start.8
  104.4 6.0 %copy-start.7 = (f32[3072,24]{0,1:T(8,128)S(1)}, f32[3072,24]{0,1:T(8,128)}, u32[]{:S(2)}) copy-start(f32[3072,24]{0,1:T(8,128)} %copy.13) | copy-start | bytes 884740
  104.4 6.8 %copy-start.6 = (f32[3072,24]{0,1:T(8,128)S(1)}, f32[3072,24]{0,1:T(8,128)}, u32[]{:S(2)}) copy-start(f32[3072,24]{0,1:T(8,128)} %copy.14) | copy-start | bytes 884740
  104.4 7.5 %copy-start.5 = (f32[3072,24]{0,1:T(8,128)S(1)}, f32[3072,24]{0,1:T(8,128)}, u32[]{:S(2)}) copy-start(f32[3072,24]{0,1:T(8,128)} %copy.15) | copy-start | bytes 884740
  113.4 37.5 %all-to-all-start = ((f32[8,3072,24]{1,2,0:T(8,128)}), f32[8,3072,24]{1,2,0:T(8,128)S(1)}, u32[]{:S(2)}, u32[]{:S(2)}) async-start(f32[8,3072,24]{1,2,0:T(8,128)} %bitcast_dynamic-update-slice_fusion), calls=%async_computation | async-start | bytes 4718592 | tf_op jit(solution)/shard_map/all_to_all | solution.py:49
  121.9 417.4 %all-gather.2.cloned.1.call-start = ((), (), s32[]{:S(2)}) async-start(), calls=%async_computation.1 | async-start | bytes 21233664 | tf_op jit(solution)/shard_map/all_gather | solution.py:75
  152.1 1.4 copy-start
  153.8 7.3 %copy-start.11 = (f32[5]{0:T(128)S(1)}, f32[5]{0:T(128)}, u32[]{:S(2)}) copy-start(f32[5]{0:T(128)} %param.7) | copy-start | bytes 64
  155.8 6.0 %collective-permute-start = (f32[8,384,2]{1,2,0:T(2,128)S(1)}, f32[8,384,2]{1,2,0:T(2,128)S(1)}, u32[]{:S(2)}, u32[]{:S(2)}) collective-permute-start(f32[8,384,2]{1,2,0:T(2,128)S(1)} %get-tuple-element.15), channel_id=1, source_target_pairs={{0,1},{1,2},{2,3},{3,4},{4,5},{5,6},{6,7},{7,8},{8,9},{9,10},{10,1... | collective-permute-start | bytes 73736 | tf_op jit(solution)/shard_map/ppermute | solution.py:18
  159.2 5.1 collective-permute-start.1
  169.2 3.1 collective-permute-start.2
  173.9 0.7 copy-start.10
  555.8 15.5 %collective-permute-start.3 = (f32[4,192,3072]{2,1,0:T(8,128)}, f32[4,192,3072]{2,1,0:T(8,128)}, u32[]{:S(2)}, u32[]{:S(2)}) collective-permute-start(f32[4,192,3072]{2,1,0:T(8,128)} %fusion.10), channel_id=1, source_target_pairs={{0,1},{1,0},{2,3},{3,2},{4,5},{5,4},{6,7},{7,6},{8,9},{9,8},{10,11... | collective-permute-start | bytes 28311560 | tf_op jit(solution)/shard_map/ppermute | solution.py:81
Sparse Core Ops, SparseCore 0:
  174.0 365.2 all-gather.1
where the time goes:
time: 595 us; the launch traced here: 594 us
  waiting for transfers between devices  386 us (65%)
  local copies, waits for them, and re-layouts  83.7 us (14%)
  other arithmetic  41.4 us (7%)
  between operations  37.4 us (6%)
  matrix products  30.1 us (5%)
  starting transfers between devices  14.9 us (3%)
    all_gather x1, waiting for transfers between devices, per_device(): right = lax.all_gather(pair, CHIPS, axis=1, tiled=True)  365 us
    gather x1, local copies, waits for them, and re-layouts, per_device(): ordered = jnp.take(block.T, pixel_order, axis=0)  43.9 us
    dot_general x2, matrix products, correlate(): jnp.einsum('rfs,rgs->rfg', left, right, precision=lax.Precision.HIGH, pre...  30.1 us
    dynamic_slice x9, local copies, waits for them, and re-layouts, per_device(): lax.dynamic_slice_in_dim(ordered, starts[d * owned], window, 0)  21.8 us
    select_n x1, other arithmetic, per_device(): jnp.where(core == 0, jnp.concatenate([mine, back], 0), jnp.concatenate([b...  15.7 us
    all_to_all x1, waiting for transfers between devices, per_device(): got = lax.all_to_all(chunks, PIX, 0, 0, tiled=True)  15.2 us
    unnamed x32, local copies, waits for them, and re-layouts  14 us
  transfers between devices with their start and end apart: 6, of which 5 were waited for; matrix products, arithmetic and copies ran while one was open for 3% of the time, Pallas kernels for 0%

commit v1 on v0

--- a/solution.py
+++ b/solution.py
@@ -72,7 +72,9 @@
     pair = jnp.where(
         core == 0, jnp.concatenate([keep, other], 1), jnp.concatenate([other, keep], 1)
     )
-    right = lax.all_gather(pair, CHIPS, axis=1, tiled=True)
+    right = jnp.concatenate(
+        lax.all_to_all(jnp.stack([pair] * lax.axis_size(CHIPS)), CHIPS, 0, 0), axis=1
+    )
     scale = lax.dynamic_slice_in_dim(cycle_sizes, me * owned + core * half, half).astype(
         jnp.float32
     )

time: 595 us -> 500 us (0.84)
  waiting for transfers between devices: 386 us -> 277 us
  local copies, waits for them, and re-layouts: 83.7 us -> 105 us
  between operations: 37.4 us -> 24.6 us
  starting transfers between devices: 14.9 us -> 21.8 us
    all_gather x1 -> x0, waiting for transfers between devices: 365 us -> none  [per_device(): right = lax.all_gather(pair, CHIPS, axis=1, tiled=True)]
    all_to_all x0 -> x1, waiting for transfers between devices: none -> 256 us  [per_device(): lax.all_to_all(jnp.stack([pair] * lax.axis_size(CHIPS)), CHIPS, 0, 0)]
    reshape x0 -> x1, local copies, waits for them, and re-layouts: none -> 12.7 us  [per_device(): jnp.concatenate(lax.all_to_all(jnp.stack([pair] * lax.axis_size(CHIPS)),...]
    another operation x1 -> x2, local copies, waits for them, and re-layouts: 0.74 us -> 9.73 us  [the longest x1 8.98 us: per_device(): jnp.stack([pair] * lax.axis_size(CHIPS))]
    all_to_all x0 -> x1, starting transfers between devices: none -> 6.47 us  [per_device(): lax.all_to_all(jnp.stack([pair] * lax.axis_size(CHIPS)), CHIPS, 0, 0)]
  transfers between devices with their start and end apart: 6 -> 6, of which waited for: 5 -> 5; matrix products, arithmetic and copies ran while one was open for 3% -> 4% of each run, Pallas kernels for 0% -> 0%
where the time goes in v1:
time: 500 us; the launch traced here: 498 us
  waiting for transfers between devices  277 us (55%)
  local copies, waits for them, and re-layouts  105 us (21%)
  other arithmetic  40.1 us (8%)
  matrix products  30.1 us (6%)
  between operations  24.6 us (5%)
  starting transfers between devices  21.8 us (4%)
    all_to_all x1, waiting for transfers between devices, per_device(): lax.all_to_all(jnp.stack([pair] * lax.axis_size(CHIPS)), CHIPS, 0, 0)  256 us
    gather x1, local copies, waits for them, and re-layouts, per_device(): ordered = jnp.take(block.T, pixel_order, axis=0)  44.1 us
    dot_general x2, matrix products, correlate(): jnp.einsum('rfs,rgs->rfg', left, right, precision=lax.Precision.HIGH, pre...  30.1 us
    dynamic_slice x9, local copies, waits for them, and re-layouts, per_device(): lax.dynamic_slice_in_dim(ordered, starts[d * owned], window, 0)  21.8 us
    select_n x1, other arithmetic, per_device(): jnp.where(core == 0, jnp.concatenate([mine, back], 0), jnp.concatenate([b...  15.7 us
    all_to_all x1, waiting for transfers between devices, per_device(): got = lax.all_to_all(chunks, PIX, 0, 0, tiled=True)  14.7 us
    unnamed x32, local copies, waits for them, and re-layouts  13.4 us
    reshape x1, local copies, waits for them, and re-layouts, per_device(): jnp.concatenate(lax.all_to_all(jnp.stack([pair] * lax.axis_size(CHIPS)),...  12.7 us
  transfers between devices with their start and end apart: 6, of which 5 were waited for; matrix products, arithmetic and copies ran while one was open for 4% of the time, Pallas kernels for 0%

profile of v1, /device:TPU:1, one launch (start us, length us, event | category | flops | bytes accessed | tf_op | source)
XLA Modules:
  0.0 498.5 jit_solution(17329274964172509540)
XLA Ops:
  0.0 0.7 copy.27
  0.8 0.1 reduce.1
  0.9 0.7 sub.49
  1.6 1.7 fusion.42
  13.3 0.8 compare_and_fusion
  14.1 0.8 fusion.39
  15.0 4.9 copy.26
  24.8 44.1 %gather_fusion = f32[12288,24]{1,0:T(8,128)} fusion(f32[12288,24]{1,0:T(8,128)} %bitcast.93, s32[12288]{0:T(1024)S(1)} %fusion.39), kind=kCustom, calls=%fused_computation | custom fusion | bytes 2408448 | tf_op jit(solution)/shard_map/jit(_take)/gather | solution.py:44
  68.9 8.6 %broadcast_select_fusion = f32[12288,24]{1,0:T(8,128)S(1)} fusion(f32[12288,24]{1,0:T(8,128)} %gather_fusion, pred[12288]{0:T(1024)(128)(4,1)S(1)} %compare_and_fusion), kind=kLoop, calls=%fused_computation.10 | loop fusion | flops 294912 | bytes 2371584 | tf_op jit(solution)/shard_map/jit(_take)/select_n | solution.py:44
  77.5 7.3 %pad_dynamic-slice_fusion = (f32[3072,24]{1,0:T(8,128)}, f32[3072,24]{1,0:T(8,128)}, f32[3072,24]{1,0:T(8,128)}, f32[3072,24]{1,0:T(8,128)}, f32[3072,24]{1,0:T(...) fusion(s32[]{:T(128)S(6)} %select_n.151, f32[12288,24]{1,0:T(8,128)S(1)} %broadcast_select_fusion, ...), kind=kLoop, calls=%fused_computation.2 | loop fusion | bytes 3538976 | tf_op jit(solution)/shard_map/dynamic_slice | solution.py:47
  84.8 2.0 copy.35
  86.8 2.6 copy.29
  89.3 1.2 copy.30
  90.5 1.2 copy.31
  91.7 2.7 copy.32
  94.4 2.6 copy.33
  97.0 1.2 copy.34
  98.1 1.2 copy.28
  99.3 1.7 bitcast_dynamic-update-slice_fusion.7
  101.0 1.7 bitcast_dynamic-update-slice_fusion.6
  102.7 0.7 bitcast_dynamic-update-slice_fusion.5
  103.4 0.7 bitcast_dynamic-update-slice_fusion.4
  104.2 0.7 bitcast_dynamic-update-slice_fusion.3
  104.9 0.7 bitcast_dynamic-update-slice_fusion.2
  105.6 0.7 bitcast_dynamic-update-slice_fusion.1
  106.4 0.7 bitcast_dynamic-update-slice_fusion
  107.1 8.5 %all-to-all-start = ((f32[8,3072,24]{1,2,0:T(8,128)}), f32[8,3072,24]{1,2,0:T(8,128)S(1)}, u32[]{:S(2)}, u32[]{:S(2)}) async-start(f32[8,3072,24]{1,2,0:T(8,128)} %bitcast_dynamic-update-slice_fusion), calls=%async_computation | async-start | bytes 4718592 | tf_op jit(solution)/shard_map/all_to_all | solution.py:49
  124.9 0.6 iota_compare_fusion
  125.6 0.6 iota_compare_fusion.1
  126.2 0.5 iota_compare_fusion.2
  126.7 0.6 iota_compare_fusion.3
  127.3 0.6 iota_compare_fusion.4
  128.0 0.6 iota_compare_fusion.5
  128.6 0.7 iota_compare_fusion.6
  129.3 0.6 iota_compare_fusion.7
  129.9 14.7 %all-to-all-done = f32[8,3072,24]{1,2,0:T(8,128)S(1)} async-done(((f32[8,3072,24]{1,2,0:T(8,128)}), f32[8,3072,24]{1,2,0:T(8,128)S(1)}, u32[]{:S(2)}, u32[]{:S(2)}) %all-to-all-start) | async-done | bytes 2359328 | tf_op jit(solution)/shard_map/all_to_all | solution.py:49
  144.6 0.2 fusion.18
  144.8 0.2 fusion.21
  145.0 0.2 fusion.24
  145.1 0.2 fusion.27
  145.3 0.2 fusion.30
  145.4 0.2 fusion.33
  145.6 0.2 fusion.36
  145.8 1.4 copy-done
  147.2 0.3 bitcast_reduce_fusion
  147.5 2.0 bitcast_divide_fusion
  149.5 3.4 collective-permute-start
  152.9 1.9 collective-permute-start.1
  154.8 0.7 fusion.41
  155.5 2.5 collective-permute-done.1
  158.0 4.7 fusion.3
  162.8 0.2 dynamic-slice_bitcast_fusion.1
  163.0 0.3 collective-permute-start.2
  163.2 2.8 collective-permute-done.2
  166.1 0.2 maximum_select_fusion.1
  166.2 9.0 %stack.83 = f32[8,4,384,384]{3,2,1,0:T(8,128)} broadcast(f32[4,384,384]{2,1,0:T(8,128)S(1)} %maximum_select_fusion.1), dimensions={1,2,3} | broadcast | bytes 21233664 | tf_op jit(solution)/shard_map/stack | solution.py:76
  175.2 6.5 %all-to-all-start.1 = ((f32[8,4,384,384]{3,2,1,0:T(8,128)}), f32[8,4,384,384]{3,2,1,0:T(8,128)}, u32[]{:S(2)}, u32[]{:S(2)}) async-start(f32[8,4,384,384]{3,2,1,0:T(8,128)} %stack.83), calls=%async_computation.1 | async-start | bytes 37748736 | tf_op jit(solution)/shard_map/all_to_all | solution.py:76
  181.8 255.8 %all-to-all-done.1 = f32[8,4,384,384]{3,2,1,0:T(8,128)} async-done(((f32[8,4,384,384]{3,2,1,0:T(8,128)}), f32[8,4,384,384]{3,2,1,0:T(8,128)}, u32[]{:S(2)}, u32[]{:S(2)}) %all-to-all-start.1) | async-done | bytes 18874400 | tf_op jit(solution)/shard_map/all_to_all | solution.py:76
  437.6 12.7 %copy.36 = f32[4,8,384,384]{3,2,1,0:T(8,128)} copy(f32[4,8,384,384]{3,2,0,1:T(8,128)} %bitcast.51) | data formatting | bytes 37748736 | tf_op jit(solution)/shard_map/reshape | solution.py:75
  450.3 16.5 %fusion.10 = f32[4,192,3072]{2,1,0:T(8,128)} fusion(f32[4,3072,384]{2,1,0:T(8,128)} %bitcast.94, f32[4,192,384]{2,1,0:T(8,128)S(1)} %collective-permute-done.2, f32[4]{0:T(128)S(1)} %dynamic-slice_convert_fusion), kind=kOutput, calls=%fused_computation.37 | convolution fusion | flops 5436112896 | bytes 29491216 | tf_op jit(solution)/shard_map/rfs,rgs->rfg/dot_general | solution.py:24
  466.8 1.3 collective-permute-start.3
  468.1 13.6 %fusion.12 = f32[4,192,3072]{2,1,0:T(8,128)S(1)} fusion(f32[4,3072,384]{2,1,0:T(8,128)} %bitcast.95, f32[4,192,384]{2,1,0:T(8,128)S(1)} %get-tuple-element.13, f32[4]{0:T(128)S(1)} %dynamic-slice_convert_fusion), kind=kOutput, calls=%fused_computation.40 | convolution fusion | flops 5436112896 | bytes 29491216 | tf_op jit(solution)/shard_map/rfs,rgs->rfg/dot_general | solution.py:24
  481.7 1.1 collective-permute-done.3
  482.7 15.7 %maximum_select_fusion = f32[8,192,3072]{2,1,0:T(8,128)} fusion(f32[4,192,3072]{2,1,0:T(8,128)} %collective-permute-done.3, f32[4,192,3072]{2,1,0:T(8,128)S(1)} %fusion.12, pred[]{:T(512)S(6)} %eq.4), kind=kLoop, calls=%fused_computation.1 | loop fusion | flops 14155776 | bytes 37748736 | tf_op jit(solution)/shard_map/jit(_where)/select_n | solution.py:85
  (29 shorter events, 0.3 us)
Async XLA Ops:
  84.8 4.6 copy-start.4
  84.8 5.8 %copy-start.3 = (f32[3072,24]{1,0:T(8,128)S(1)}, f32[3072,24]{1,0:T(8,128)}, u32[]{:S(2)}) copy-start(f32[3072,24]{1,0:T(8,128)} %get-tuple-element.8) | copy-start | bytes 884740
  90.5 6.4 %copy-start.2 = (f32[3072,24]{1,0:T(8,128)S(1)}, f32[3072,24]{1,0:T(8,128)}, u32[]{:S(2)}) copy-start(f32[3072,24]{1,0:T(8,128)} %get-tuple-element.11) | copy-start | bytes 884740
  91.7 6.4 %copy-start.1 = (f32[3072,24]{1,0:T(8,128)S(1)}, f32[3072,24]{1,0:T(8,128)}, u32[]{:S(2)}) copy-start(f32[3072,24]{1,0:T(8,128)} %get-tuple-element.12) | copy-start | bytes 884740
  98.1 4.6 copy-start.9
  98.1 5.3 %copy-start.8 = (f32[3072,24]{0,1:T(8,128)S(1)}, f32[3072,24]{0,1:T(8,128)}, u32[]{:S(2)}) copy-start(f32[3072,24]{0,1:T(8,128)} %copy.31) | copy-start | bytes 884740
  98.1 6.1 %copy-start.7 = (f32[3072,24]{0,1:T(8,128)S(1)}, f32[3072,24]{0,1:T(8,128)}, u32[]{:S(2)}) copy-start(f32[3072,24]{0,1:T(8,128)} %copy.32) | copy-start | bytes 884740
  98.1 6.8 %copy-start.6 = (f32[3072,24]{0,1:T(8,128)S(1)}, f32[3072,24]{0,1:T(8,128)}, u32[]{:S(2)}) copy-start(f32[3072,24]{0,1:T(8,128)} %copy.33) | copy-start | bytes 884740
  98.1 7.5 %copy-start.5 = (f32[3072,24]{0,1:T(8,128)S(1)}, f32[3072,24]{0,1:T(8,128)}, u32[]{:S(2)}) copy-start(f32[3072,24]{0,1:T(8,128)} %copy.34) | copy-start | bytes 884740
  107.1 37.5 %all-to-all-start = ((f32[8,3072,24]{1,2,0:T(8,128)}), f32[8,3072,24]{1,2,0:T(8,128)S(1)}, u32[]{:S(2)}, u32[]{:S(2)}) async-start(f32[8,3072,24]{1,2,0:T(8,128)} %bitcast_dynamic-update-slice_fusion), calls=%async_computation | async-start | bytes 4718592 | tf_op jit(solution)/shard_map/all_to_all | solution.py:49
  145.8 1.4 copy-start
  147.5 7.3 %copy-start.11 = (f32[5]{0:T(128)S(1)}, f32[5]{0:T(128)}, u32[]{:S(2)}) copy-start(f32[5]{0:T(128)} %param.7) | copy-start | bytes 64
  149.5 6.0 %collective-permute-start = (f32[8,384,2]{1,2,0:T(2,128)S(1)}, f32[8,384,2]{1,2,0:T(2,128)S(1)}, u32[]{:S(2)}, u32[]{:S(2)}) collective-permute-start(f32[8,384,2]{1,2,0:T(2,128)S(1)} %get-tuple-element.15), channel_id=1, source_target_pairs={{0,1},{1,2},{2,3},{3,4},{4,5},{5,6},{6,7},{7,8},{8,9},{9,10},{10,1... | collective-permute-start | bytes 73736 | tf_op jit(solution)/shard_map/ppermute | solution.py:18
  152.9 5.1 %collective-permute-start.1 = (f32[8,384,2]{1,2,0:T(2,128)S(1)}, f32[8,384,2]{1,2,0:T(2,128)S(1)}, u32[]{:S(2)}, u32[]{:S(2)}) collective-permute-start(f32[8,384,2]{1,2,0:T(2,128)S(1)} %get-tuple-element.16), channel_id=1, source_target_pairs={{1,0},{2,1},{3,2},{4,3},{5,4},{6,5},{7,6},{8,7},{9,8},{10,9},{11,1... | collective-permute-start | bytes 73736 | tf_op jit(solution)/shard_map/ppermute | solution.py:19
  163.0 3.1 collective-permute-start.2
  175.2 6.5 %copy-start.10 = (s32[64]{0:T(128)S(1)}, s32[64]{0:T(128)}, u32[]{:S(2)}) copy-start(s32[64]{0:T(128)} %param.6) | copy-start | bytes 772
  175.2 262.4 %all-to-all-start.1 = ((f32[8,4,384,384]{3,2,1,0:T(8,128)}), f32[8,4,384,384]{3,2,1,0:T(8,128)}, u32[]{:S(2)}, u32[]{:S(2)}) async-start(f32[8,4,384,384]{3,2,1,0:T(8,128)} %stack.83), calls=%async_computation.1 | async-start | bytes 37748736 | tf_op jit(solution)/shard_map/all_to_all | solution.py:76
  466.8 15.9 %collective-permute-start.3 = (f32[4,192,3072]{2,1,0:T(8,128)}, f32[4,192,3072]{2,1,0:T(8,128)}, u32[]{:S(2)}, u32[]{:S(2)}) collective-permute-start(f32[4,192,3072]{2,1,0:T(8,128)} %fusion.10), channel_id=1, source_target_pairs={{0,1},{1,0},{2,3},{3,2},{4,5},{5,4},{6,7},{7,6},{8,9},{9,8},{10,11... | collective-permute-start | bytes 28311560 | tf_op jit(solution)/shard_map/ppermute | solution.py:83
